TPU v7x, 256 devices: a whole 4x4x8 slice. The times are simulated.
256 devices in a mesh: dp: 32 (over y, x, core), tensor: 8 (over z).
Axes of the slice: x: 4, y: 4, z: 8, core: 2. Of those that a mesh axis runs over, the one named last changes fastest.
Arguments:
- tokens: bfloat16 [8192, 8192], P('dp'), may hold values from -6 to 6
- router_weight: bfloat16 [8192, 32], replicated, may hold values from -0.0625 to 0.0625
- gate_weight: bfloat16 [14336, 8192], P(('dp', 'tensor')), may hold values from -0.0625 to 0.0625
- up_weight: bfloat16 [14336, 8192], P(('dp', 'tensor')), may hold values from -0.0625 to 0.0625
- down_weight: bfloat16 [14336, 8192], P(('dp', 'tensor')), may hold values from -0.25 to 0.25
- cluster_of: int32 [14336, 1], P('dp'), may hold values from 0 to 31; in each aligned block of 448 rows (0 to 447, 448 to 895, ...) at most 28 rows name the same one
- expert_ids: int32 [8192, 2], P('dp'), may hold values from 0 to 31, all different within a row; in each aligned block of 256 rows (0 to 255, 256 to 511, ...) at most 32 rows name the same one
Outputs:
- mixed_out: bfloat16 [8192, 8192], P('dp', 'tensor')
Inputs may be any that keep to these rules, and one draw needn't show every extreme that they name: `expert_ids`: in each aligned block of 256 rows (the tokens of one dp index) no expert is named by more than 32 rows, a bound that some block reaches; a row names two different experts; every expert is named somewhere. `cluster_of`: in each aligned block of 448 hidden units no cluster holds more than 28 units, and some cluster holds exactly 28; every cluster holds some unit.
All inputs are finite; a program needn't handle non-finite values.
Results may differ from a plain program's by a relative error of at most 0.023.
Values may be sent and summed in bfloat16 or wider, within the bound.
No kernel may reach another device: no remote copies, remote signals or barrier semaphores. Data moves between devices by JAX's collectives and lax.ppermute only.
A program may use at most 64 MiB of HBM per device.

v0:
```python
import jax
import jax.numpy as jnp
from jax import lax
from jax.sharding import PartitionSpec as P


def place_rows(labels, bin_count, capacity):
    count_rows = labels.shape[0]
    onehot = (labels[:, None] == jnp.arange(bin_count, dtype=jnp.int32)[None, :]).astype(jnp.int32)
    before = jnp.cumsum(onehot, axis=0) - onehot
    rank_in = jnp.sum(before * onehot, axis=1)
    position = labels * capacity + rank_in
    slot_list = jnp.full((bin_count * capacity,), count_rows, jnp.int32)
    slot_list = slot_list.at[position].set(jnp.arange(count_rows, dtype=jnp.int32))
    return (slot_list, position)


def with_zero_row(matrix):
    return jnp.concatenate([matrix, jnp.zeros((1, matrix.shape[1]), matrix.dtype)], axis=0)


def against(left_side, right_side):
    return lax.dot_general(
        left_side, right_side, (((1,), (1,)), ((), ())), preferred_element_type=jnp.float32
    )


def on_device(tokens, router_weight, gate_weight, up_weight, down_weight, cluster_of, expert_ids):
    owners = lax.axis_size("dp")
    tensor_count = lax.axis_size("tensor")
    width_part = tokens.shape[1] // tensor_count
    token_count = tokens.shape[0]
    gate_rows, up_rows, down_rows = (
        lax.all_to_all(gate_weight, "tensor", split_axis=1, concat_axis=0, tiled=True),
        lax.all_to_all(up_weight, "tensor", split_axis=1, concat_axis=0, tiled=True),
        lax.all_to_all(down_weight, "tensor", split_axis=1, concat_axis=0, tiled=True),
    )
    unit_cap = 2 * gate_rows.shape[0] // owners
    unit_list, unit_spot = place_rows(cluster_of[:, 0], owners, unit_cap)
    gate_pick = with_zero_row(gate_rows)[unit_list]
    up_pick = with_zero_row(up_rows)[unit_list]
    down_pick = with_zero_row(down_rows)[unit_list]
    gate_own, up_own, down_own = (
        lax.all_to_all(gate_pick, "dp", split_axis=0, concat_axis=0, tiled=True),
        lax.all_to_all(up_pick, "dp", split_axis=0, concat_axis=0, tiled=True),
        lax.all_to_all(down_pick, "dp", split_axis=0, concat_axis=0, tiled=True),
    )
    capacity = 4 * token_count // owners
    flat_ids = expert_ids.reshape(-1)
    slot_list, slot_spot = place_rows(flat_ids, owners, capacity)
    features = lax.dynamic_slice_in_dim(
        tokens, lax.axis_index("tensor") * width_part, width_part, 1
    )
    outgoing = with_zero_row(features)[slot_list // 2]
    arrived = lax.all_to_all(outgoing, "dp", split_axis=0, concat_axis=0, tiled=True)
    gate_part = against(arrived, gate_own)
    up_part = against(arrived, up_own)
    gate_sum, up_sum = (
        lax.psum(gate_part.astype(jnp.bfloat16), "tensor").astype(jnp.float32),
        lax.psum(up_part.astype(jnp.bfloat16), "tensor").astype(jnp.float32),
    )
    hidden = (jax.nn.silu(gate_sum) * up_sum).astype(jnp.bfloat16)
    expert_out = jnp.dot(hidden, down_own, preferred_element_type=jnp.float32).astype(jnp.bfloat16)
    returned = lax.all_to_all(expert_out, "dp", split_axis=0, concat_axis=0, tiled=True)
    picked_out = returned[slot_spot].reshape(token_count, 2, width_part)
    logits = jnp.dot(tokens, router_weight, preferred_element_type=jnp.float32)
    scores = jax.nn.sigmoid(jnp.take_along_axis(logits, expert_ids, axis=1))
    mixing = scores / jnp.sum(scores, axis=1, keepdims=True)
    mixed_out = jnp.sum(mixing[:, :, None] * picked_out.astype(jnp.float32), axis=1)
    return mixed_out.astype(jnp.bfloat16)


def solution(mesh):
    in_specs = (
        P("dp", None),
        P(),
        P(("dp", "tensor"), None),
        P(("dp", "tensor"), None),
        P(("dp", "tensor"), None),
        P("dp", None),
        P("dp", None),
    )
    out_specs = P("dp", "tensor")
    return jax.shard_map(
        on_device, mesh=mesh, in_specs=in_specs, out_specs=out_specs, check_vma=False
    )
```

profile of v0, /device:TPU:1, one launch (start us, length us, event | category | flops | bytes accessed | tf_op | source)
XLA Modules:
  0.0 355.5 jit_solution(3648247955908489154)
XLA Ops:
  8.9 9.0 %all-to-all-start.3 = ((bf16[56,8,1024]{2,0,1:T(8,128)(2,1)}), bf16[56,8,1024]{2,0,1:T(8,128)(2,1)S(1)}, u32[]{:S(2)}, u32[]{:S(2)}) async-start(bf16[56,8,1024]{2,0,1:T(8,128)(2,1)} %bitcast.70), calls=%async_computation.3 | async-start | bytes 1835008 | tf_op jit(solution)/shard_map/all_to_all | solution.py:35
  18.9 25.4 %all-to-all-done.3 = bf16[56,8,1024]{2,0,1:T(8,128)(2,1)S(1)} async-done(((bf16[56,8,1024]{2,0,1:T(8,128)(2,1)}), bf16[56,8,1024]{2,0,1:T(8,128)(2,1)S(1)}, u32[]{:S(2)}, u32[]{:S(2)}) %all-to-all-start.3) | async-done | bytes 917536 | tf_op jit(solution)/shard_map/all_to_all | solution.py:35
  44.2 3.6 all-to-all-start.1
  54.2 5.4 %gather_fusion = bf16[1024,1024]{1,0:T(8,128)(2,1)} fusion(bf16[257,1024]{1,0:T(8,128)(2,1)S(1)} %concatenate.12, s32[1024]{0:T(1024)S(1)} %fusion.13), kind=kCustom, calls=%fused_computation | custom fusion | bytes 4198400 | tf_op jit(solution)/shard_map/gather | solution.py:54
  59.6 14.5 %all-to-all-done.1 = bf16[56,8,1024]{2,0,1:T(8,128)(2,1)S(1)} async-done(((bf16[56,8,1024]{2,0,1:T(8,128)(2,1)}), bf16[56,8,1024]{2,0,1:T(8,128)(2,1)S(1)}, u32[]{:S(2)}, u32[]{:S(2)}) %all-to-all-start.1) | async-done | bytes 917536 | tf_op jit(solution)/shard_map/all_to_all | solution.py:34
  75.0 7.6 %all-to-all-start = ((bf16[32,32,1024]{2,1,0:T(8,128)(2,1)}), bf16[32,32,1024]{2,1,0:T(8,128)(2,1)}, u32[]{:S(2)}, u32[]{:S(2)}) async-start(bf16[32,32,1024]{2,1,0:T(8,128)(2,1)} %bitcast.4), calls=%async_computation | async-start | bytes 4194304 | tf_op jit(solution)/shard_map/all_to_all | solution.py:55
  87.3 3.6 %gather_fusion.2 = bf16[896,1024]{1,0:T(8,128)(2,1)S(1)} fusion(bf16[449,1024]{1,0:T(8,128)(2,1)S(1)} %concatenate.14, s32[1024]{0:T(1024)S(1)} %pad_clamp_fusion.1), kind=kCustom, calls=%fused_computation.2 | custom fusion | bytes 3673600 | tf_op jit(solution)/shard_map/gather | solution.py:41
  92.5 18.9 %all-to-all-done = bf16[32,32,1024]{2,1,0:T(8,128)(2,1)} async-done(((bf16[32,32,1024]{2,1,0:T(8,128)(2,1)}), bf16[32,32,1024]{2,1,0:T(8,128)(2,1)}, u32[]{:S(2)}, u32[]{:S(2)}) %all-to-all-start) | async-done | bytes 2097184 | tf_op jit(solution)/shard_map/all_to_all | solution.py:55
  111.4 5.3 %all-to-all-start.4 = ((bf16[32,28,1024]{2,1,0:T(8,128)(2,1)}), bf16[32,28,1024]{2,1,0:T(8,128)(2,1)S(1)}, u32[]{:S(2)}, u32[]{:S(2)}) async-start(bf16[32,28,1024]{2,1,0:T(8,128)(2,1)} %all_to_all.96), calls=%async_computation.4 | async-start | bytes 4194304 | tf_op jit(solution)/shard_map/all_to_all | solution.py:45
  117.9 4.4 %gather_fusion.1 = bf16[896,1024]{1,0:T(8,128)(2,1)} fusion(bf16[449,1024]{1,0:T(8,128)(2,1)S(1)} %concatenate.13, s32[1024]{0:T(1024)} %copy-done.4), kind=kCustom, calls=%fused_computation.1 | custom fusion | bytes 3673600 | tf_op jit(solution)/shard_map/gather | solution.py:40
  122.3 3.7 %all_to_all.89 = bf16[32,28,1024]{2,1,0:T(8,128)(2,1)} reshape(bf16[896,1024]{1,0:T(8,128)(2,1)} %gather_fusion.1) | data formatting | bytes 3670016 | tf_op jit(solution)/shard_map/all_to_all | solution.py:44
  126.0 19.0 %all-to-all-done.4 = bf16[32,28,1024]{2,1,0:T(8,128)(2,1)S(1)} async-done(((bf16[32,28,1024]{2,1,0:T(8,128)(2,1)}), bf16[32,28,1024]{2,1,0:T(8,128)(2,1)S(1)}, u32[]{:S(2)}, u32[]{:S(2)}) %all-to-all-start.4) | async-done | bytes 1835040 | tf_op jit(solution)/shard_map/all_to_all | solution.py:45
  145.0 6.5 %all-to-all-start.2 = ((bf16[32,28,1024]{2,1,0:T(8,128)(2,1)}), bf16[32,28,1024]{2,1,0:T(8,128)(2,1)}, u32[]{:S(2)}, u32[]{:S(2)}) async-start(bf16[32,28,1024]{2,1,0:T(8,128)(2,1)} %all_to_all.89), calls=%async_computation.2 | async-start | bytes 4194304 | tf_op jit(solution)/shard_map/all_to_all | solution.py:44
  153.2 5.7 %convolution_convert_fusion.1 = bf16[1024,896]{1,0:T(8,128)(2,1)} fusion(bf16[1024,1024]{1,0:T(8,128)(2,1)} %bitcast.5, bf16[896,1024]{1,0:T(8,128)(2,1)} %all_to_all.98), kind=kOutput, calls=%fused_computation.17 | convolution fusion | flops 1879965696 | bytes 5767168 | tf_op jit(solution)/shard_map/dot_general | solution.py:23
  159.0 20.9 %all-to-all-done.2 = bf16[32,28,1024]{2,1,0:T(8,128)(2,1)} async-done(((bf16[32,28,1024]{2,1,0:T(8,128)(2,1)}), bf16[32,28,1024]{2,1,0:T(8,128)(2,1)}, u32[]{:S(2)}, u32[]{:S(2)}) %all-to-all-start.2) | async-done | bytes 1835040 | tf_op jit(solution)/shard_map/all_to_all | solution.py:44
  182.4 5.3 %convolution_convert_fusion.2 = bf16[1024,896]{1,0:T(8,128)(2,1)} fusion(bf16[1024,1024]{1,0:T(8,128)(2,1)} %bitcast.5, bf16[896,1024]{1,0:T(8,128)(2,1)S(1)} %all_to_all.91), kind=kOutput, calls=%fused_computation.18 | convolution fusion | flops 1879965696 | bytes 5767168 | tf_op jit(solution)/shard_map/dot_general | solution.py:23
  188.9 37.4 %all_to_all.117 = bf16[56,8,1024]{2,0,1:T(8,128)(2,1)S(1)} all-to-all(bf16[56,8,1024]{2,0,1:T(8,128)(2,1)S(1)} %bitcast.73), channel_id=1, replica_groups=mesh['dp'=32,'tensor'=8] {'tensor'}, dimensions={1} | all-to-all | bytes 1835008 | tf_op jit(solution)/shard_map/all_to_all | solution.py:36
  226.4 4.2 %gather_fusion.3 = bf16[896,1024]{1,0:T(8,128)(2,1)} fusion(bf16[449,1024]{1,0:T(8,128)(2,1)S(1)} %concatenate.15, s32[1024]{0:T(1024)S(1)} %copy-done.5), kind=kCustom, calls=%fused_computation.3 | custom fusion | bytes 3673600 | tf_op jit(solution)/shard_map/gather | solution.py:42
  233.1 34.4 %all_to_all.118 = bf16[32,28,1024]{2,1,0:T(8,128)(2,1)} all-to-all(bf16[32,28,1024]{2,1,0:T(8,128)(2,1)S(1)} %all_to_all.103), channel_id=1, replica_groups=mesh['dp'=32,'tensor'=8] {'dp'}, dimensions={0} | all-to-all | bytes 3670016 | tf_op jit(solution)/shard_map/all_to_all | solution.py:46
  270.0 27.6 %all-reduce.8.cloned.1.call-done = (bf16[1024,896]{1,0:T(8,128)(2,1)}, bf16[1024,896]{1,0:T(8,128)(2,1)}) async-done(((bf16[1024,896]{1,0:T(8,128)(2,1)}, bf16[1024,896]{1,0:T(8,128)(2,1)}), (bf16[1024,896]{1,0:T(8,128)(2,1)}, bf16[1024,896]{1,0:T(8,128)(2,1)})) %all-reduce.8.cloned.1.call-update) | async-done | bytes 3670032 | tf_op jit(solution)/shard_map/psum | solution.py:60
  297.6 6.0 %convolution_convert_fusion = bf16[1024,1024]{1,0:T(8,128)(2,1)} fusion(bf16[896,1024]{1,0:T(8,128)(2,1)S(1)} %all_to_all.105, bf16[1024,896]{1,0:T(8,128)(2,1)} %get-tuple-element.5, bf16[1024,896]{1,0:T(8,128)(2,1)} %get-tuple-element.6), kind=kOutput, calls=%fused_computation.16 | convolution fusion | flops 1887436800 | bytes 7602176 | tf_op jit(solution)/shard_map/dot_general | solution.py:63
  303.6 7.8 %all-to-all-start.7 = ((bf16[32,32,1024]{2,1,0:T(8,128)(2,1)}), bf16[32,32,1024]{2,1,0:T(8,128)(2,1)S(1)}, u32[]{:S(2)}, u32[]{:S(2)}) async-start(bf16[32,32,1024]{2,1,0:T(8,128)(2,1)} %bitcast.77), calls=%async_computation.7 | async-start | bytes 4194304 | tf_op jit(solution)/shard_map/all_to_all | solution.py:64
  315.3 4.5 %gather_fusion.5 = f32[512]{0:T(512)S(1)} fusion(f32[256,32]{0,1:T(8,128)S(1)} %fusion.21, s32[512]{0:T(512)S(1)} %reshape.150), kind=kCustom, calls=%fused_computation.5 | custom fusion | bytes 8192 | tf_op jit(solution)/shard_map/jit(take_along_axis)/gather | solution.py:67
  320.3 19.6 %all-to-all-done.7 = bf16[32,32,1024]{2,1,0:T(8,128)(2,1)S(1)} async-done(((bf16[32,32,1024]{2,1,0:T(8,128)(2,1)}), bf16[32,32,1024]{2,1,0:T(8,128)(2,1)S(1)}, u32[]{:S(2)}, u32[]{:S(2)}) %all-to-all-start.7) | async-done | bytes 2097184 | tf_op jit(solution)/shard_map/all_to_all | solution.py:64
  (79 shorter events, 41.3 us)
Async XLA Ops:
  6.5 305.2 %copy-start = (bf16[8192,32]{0,1:T(8,128)(2,1)S(1)}, bf16[8192,32]{0,1:T(8,128)(2,1)}, u32[]{:S(2)}) copy-start(bf16[8192,32]{0,1:T(8,128)(2,1)} %param.8) | copy-start | bytes 1572868
  6.5 11.3 %copy-start.2 = (bf16[56,8192]{1,0:T(8,128)(2,1)S(1)}, bf16[56,8192]{1,0:T(8,128)(2,1)}, u32[]{:S(2)}) copy-start(bf16[56,8192]{1,0:T(8,128)(2,1)} %param.9) | copy-start | bytes 2752516
  8.9 35.4 %all-to-all-start.3 = ((bf16[56,8,1024]{2,0,1:T(8,128)(2,1)}), bf16[56,8,1024]{2,0,1:T(8,128)(2,1)S(1)}, u32[]{:S(2)}, u32[]{:S(2)}) async-start(bf16[56,8,1024]{2,0,1:T(8,128)(2,1)} %bitcast.70), calls=%async_computation.3 | async-start | bytes 1835008 | tf_op jit(solution)/shard_map/all_to_all | solution.py:35
  17.9 29.9 %copy-start.6 = (s32[256,2]{0,1:T(2,128)S(1)}, s32[256,2]{0,1:T(2,128)}, u32[]{:S(2)}) copy-start(s32[256,2]{0,1:T(2,128)} %param.13) | copy-start | bytes 6148
  44.2 29.9 %all-to-all-start.1 = ((bf16[56,8,1024]{2,0,1:T(8,128)(2,1)}), bf16[56,8,1024]{2,0,1:T(8,128)(2,1)S(1)}, u32[]{:S(2)}, u32[]{:S(2)}) async-start(bf16[56,8,1024]{2,0,1:T(8,128)(2,1)} %bitcast.71), calls=%async_computation.1 | async-start | bytes 1835008 | tf_op jit(solution)/shard_map/all_to_all | solution.py:34
  51.3 0.5 copy-start.9
  74.1 0.9 copy-start.1
  74.1 8.6 %copy-start.8 = (s32[448,1]{0,1:T(1,128)S(1)}, s32[448,1]{0,1:T(1,128)}, u32[]{:S(2)}) copy-start(s32[448,1]{0,1:T(1,128)} %param.12) | copy-start | bytes 5380
  75.0 36.4 %all-to-all-start = ((bf16[32,32,1024]{2,1,0:T(8,128)(2,1)}), bf16[32,32,1024]{2,1,0:T(8,128)(2,1)}, u32[]{:S(2)}, u32[]{:S(2)}) async-start(bf16[32,32,1024]{2,1,0:T(8,128)(2,1)} %bitcast.4), calls=%async_computation | async-start | bytes 4194304 | tf_op jit(solution)/shard_map/all_to_all | solution.py:55
  87.3 3.7 %copy-start.4 = (s32[1024]{0:T(1024)}, s32[1024]{0:T(1024)S(1)}, u32[]{:S(2)}) copy-start(s32[1024]{0:T(1024)S(1)} %pad_clamp_fusion.1) | copy-start | bytes 12292
  111.4 33.6 %all-to-all-start.4 = ((bf16[32,28,1024]{2,1,0:T(8,128)(2,1)}), bf16[32,28,1024]{2,1,0:T(8,128)(2,1)S(1)}, u32[]{:S(2)}, u32[]{:S(2)}) async-start(bf16[32,28,1024]{2,1,0:T(8,128)(2,1)} %all_to_all.96), calls=%async_computation.4 | async-start | bytes 4194304 | tf_op jit(solution)/shard_map/all_to_all | solution.py:45
  145.0 34.9 %all-to-all-start.2 = ((bf16[32,28,1024]{2,1,0:T(8,128)(2,1)}), bf16[32,28,1024]{2,1,0:T(8,128)(2,1)}, u32[]{:S(2)}, u32[]{:S(2)}) async-start(bf16[32,28,1024]{2,1,0:T(8,128)(2,1)} %all_to_all.89), calls=%async_computation.2 | async-start | bytes 4194304 | tf_op jit(solution)/shard_map/all_to_all | solution.py:44
  151.5 146.1 %all-reduce.8.cloned.1.call-start = ((), (), s32[]{:S(2)}) async-start(), calls=%async_computation.8 | async-start | bytes 7340032 | tf_op jit(solution)/shard_map/psum | solution.py:60
  187.6 1.2 copy-start.3
  188.9 37.5 %copy-start.5 = (s32[1024]{0:T(1024)S(1)}, s32[1024]{0:T(1024)}, u32[]{:S(2)}) copy-start(s32[1024]{0:T(1024)} %copy-done.4) | copy-start | bytes 12292
  303.6 7.8 %copy-start.7 = (s32[256,2]{0,1:T(2,128)S(1)}, s32[256,2]{0,1:T(2,128)}, u32[]{:S(2)}) copy-start(s32[256,2]{0,1:T(2,128)} %param.13) | copy-start | bytes 6148
  303.6 36.4 %all-to-all-start.7 = ((bf16[32,32,1024]{2,1,0:T(8,128)(2,1)}), bf16[32,32,1024]{2,1,0:T(8,128)(2,1)S(1)}, u32[]{:S(2)}, u32[]{:S(2)}) async-start(bf16[32,32,1024]{2,1,0:T(8,128)(2,1)} %bitcast.77), calls=%async_computation.7 | async-start | bytes 4194304 | tf_op jit(solution)/shard_map/all_to_all | solution.py:64
  315.3 5.0 %copy-start.10 = (s32[512,1]{0,1:T(1,128)S(1)}, s32[512,1]{0,1:T(1,128)}, u32[]{:S(2)}) copy-start(s32[512,1]{0,1:T(1,128)} %copy-done.9) | copy-start | bytes 6148
Sparse Core Ops, SparseCore 0:
  187.8 109.8 all-reduce.7
where the time goes:
time: 357 us; the launch traced here: 355 us
  waiting for transfers between devices  146 us (41%)
  blocking collectives  71.9 us (20%)
  local copies, waits for them, and re-layouts  57.1 us (16%)
  starting transfers between devices  40 us (11%)
  matrix products  20.5 us (6%)
  between operations  13.8 us (4%)
  other arithmetic  6.23 us (2%)
    all_to_all x1, blocking collectives, on_device(): lax.all_to_all(down_weight, 'tensor', split_axis=1, concat_axis=0, tiled=...  37.4 us
    all_to_all x1, blocking collectives, on_device(): lax.all_to_all(down_pick, 'dp', split_axis=0, concat_axis=0, tiled=True)  34.4 us
    psum x1, waiting for transfers between devices, on_device(): lax.psum(up_part.astype(jnp.bfloat16), 'tensor').astype(jnp.float32)  27.6 us
    all_to_all x1, waiting for transfers between devices, on_device(): lax.all_to_all(up_weight, 'tensor', split_axis=1, concat_axis=0, tiled=True)  25.4 us
    all_to_all x1, waiting for transfers between devices, on_device(): lax.all_to_all(gate_pick, 'dp', split_axis=0, concat_axis=0, tiled=True)  20.9 us
    all_to_all x1, waiting for transfers between devices, on_device(): lax.all_to_all(expert_out, 'dp', split_axis=0, concat_axis=0, tiled=True)  19.6 us
    all_to_all x1, waiting for transfers between devices, on_device(): lax.all_to_all(up_pick, 'dp', split_axis=0, concat_axis=0, tiled=True)  19 us
    all_to_all x1, waiting for transfers between devices, on_device(): lax.all_to_all(outgoing, 'dp', split_axis=0, concat_axis=0, tiled=True)  18.9 us
  transfers between devices with their start and end apart: 7, of which 7 were waited for; matrix products, arithmetic and copies ran while one was open for 13% of the time, Pallas kernels for 0%

commit v1 on v0

v1 whole, which is shorter than its diff:
```python
import jax
import jax.numpy as jnp
from jax import lax
from jax.sharding import PartitionSpec as P


def place_rows(labels, bin_count, capacity):
    count_rows = labels.shape[0]
    onehot = (labels[:, None] == jnp.arange(bin_count, dtype=jnp.int32)[None, :]).astype(jnp.int32)
    before = jnp.cumsum(onehot, axis=0) - onehot
    rank_in = jnp.sum(before * onehot, axis=1)
    position = labels * capacity + rank_in
    slot_list = jnp.full((bin_count * capacity,), count_rows, jnp.int32)
    slot_list = slot_list.at[position].set(jnp.arange(count_rows, dtype=jnp.int32))
    return (slot_list, position)


def with_zero_row(matrix):
    pad = jnp.zeros((1,) + matrix.shape[1:], matrix.dtype)
    return jnp.concatenate([matrix, pad], axis=0)


def against(left_side, right_side):
    return lax.dot_general(
        left_side, right_side, (((1,), (1,)), ((), ())), preferred_element_type=jnp.float32
    )


def on_device(tokens, router_weight, gate_weight, up_weight, down_weight, cluster_of, expert_ids):
    owners = lax.axis_size("dp")
    tensor_count = lax.axis_size("tensor")
    width_part = tokens.shape[1] // tensor_count
    token_count = tokens.shape[0]

    logits = jnp.dot(tokens, router_weight, preferred_element_type=jnp.float32)
    scores = jax.nn.sigmoid(jnp.take_along_axis(logits, expert_ids, axis=1))
    mixing = scores / jnp.sum(scores, axis=1, keepdims=True)

    stacked = jnp.stack([gate_weight, up_weight, down_weight], axis=1)
    rows = lax.all_to_all(stacked, "tensor", split_axis=2, concat_axis=0, tiled=True)
    unit_cap = 2 * rows.shape[0] // owners
    unit_list, unit_spot = place_rows(cluster_of[:, 0], owners, unit_cap)
    pick = with_zero_row(rows)[unit_list]
    own = lax.all_to_all(pick, "dp", split_axis=0, concat_axis=0, tiled=True)

    capacity = 4 * token_count // owners
    flat_ids = expert_ids.reshape(-1)
    slot_list, slot_spot = place_rows(flat_ids, owners, capacity)
    features = lax.dynamic_slice_in_dim(
        tokens, lax.axis_index("tensor") * width_part, width_part, 1
    )
    outgoing = with_zero_row(features)[slot_list // 2]
    arrived = lax.all_to_all(outgoing, "dp", split_axis=0, concat_axis=0, tiled=True)

    gate_part = against(arrived, own[:, 0, :]).astype(jnp.bfloat16)
    up_part = against(arrived, own[:, 1, :]).astype(jnp.bfloat16)
    both = jnp.stack([gate_part, up_part], axis=1)
    summed = lax.psum_scatter(both, "tensor", scatter_dimension=0, tiled=True).astype(jnp.float32)
    hidden_part = (jax.nn.silu(summed[:, 0, :]) * summed[:, 1, :]).astype(jnp.bfloat16)
    hidden = lax.all_gather(hidden_part, "tensor", axis=0, tiled=True)
    expert_out = jnp.dot(hidden, own[:, 2, :], preferred_element_type=jnp.float32).astype(jnp.bfloat16)
    returned = lax.all_to_all(expert_out, "dp", split_axis=0, concat_axis=0, tiled=True)
    picked_out = returned[slot_spot].reshape(token_count, 2, width_part)
    mixed_out = jnp.sum(mixing[:, :, None] * picked_out.astype(jnp.float32), axis=1)
    return mixed_out.astype(jnp.bfloat16)


def solution(mesh):
    in_specs = (
        P("dp", None),
        P(),
        P(("dp", "tensor"), None),
        P(("dp", "tensor"), None),
        P(("dp", "tensor"), None),
        P("dp", None),
        P("dp", None),
    )
    out_specs = P("dp", "tensor")
    return jax.shard_map(
        on_device, mesh=mesh, in_specs=in_specs, out_specs=out_specs, check_vma=False
    )
```

time: 357 us -> 452 us (1.27)
  waiting for transfers between devices: 146 us -> 246 us
  blocking collectives: 71.9 us -> 0 us
  local copies, waits for them, and re-layouts: 57.1 us -> 125 us
  other arithmetic: 6.23 us -> 12.4 us
    all_to_all x2 -> x0, blocking collectives: 71.9 us -> none  [the longest x1 37.4 us: on_device(): lax.all_to_all(down_weight, 'tensor', split_axis=1, concat_axis=0, tiled=...]
    all_to_all x4 -> x2, waiting for transfers between devices: 79.7 us -> 137 us  [the longest x1 75.9 us: on_device(): own = lax.all_to_all(pick, 'dp', split_axis=0, concat_axis=0, tiled=True)]
    reduce_scatter x0 -> x1, waiting for transfers between devices: none -> 44 us  [on_device(): lax.psum_scatter(both, 'tensor', scatter_dimension=0, tiled=True)]
    all_gather x0 -> x1, waiting for transfers between devices: none -> 35.5 us  [on_device(): hidden = lax.all_gather(hidden_part, 'tensor', axis=0, tiled=True)]
    psum x1 -> x0, waiting for transfers between devices: 27.6 us -> none  [on_device(): lax.psum(up_part.astype(jnp.bfloat16), 'tensor').astype(jnp.float32)]
    unnamed x23 -> x13, local copies, waits for them, and re-layouts: 2.76 us -> 25.7 us
    gather x3 -> x1, local copies, waits for them, and re-layouts: 12.2 us -> 33 us  [on_device(): pick = with_zero_row(rows)[unit_list]]
    slice x1 -> x2, local copies, waits for them, and re-layouts: 0.22 us -> 18.5 us  [the longest x1 18.2 us: on_device(): own[:, 2, :]]
  transfers between devices with their start and end apart: 7 -> 6, of which waited for: 7 -> 6; matrix products, arithmetic and copies ran while one was open for 13% -> 9% of each run, Pallas kernels for 0% -> 0%
where the time goes in v1:
time: 452 us; the launch traced here: 451 us
  waiting for transfers between devices  246 us (54%)
  local copies, waits for them, and re-layouts  125 us (28%)
  starting transfers between devices  37.2 us (8%)
  matrix products  16.8 us (4%)
  between operations  13.8 us (3%)
  other arithmetic  12.4 us (3%)
    all_to_all x1, waiting for transfers between devices, on_device(): own = lax.all_to_all(pick, 'dp', split_axis=0, concat_axis=0, tiled=True)  75.9 us
    all_to_all x1, waiting for transfers between devices, on_device(): lax.all_to_all(stacked, 'tensor', split_axis=2, concat_axis=0, tiled=True)  61.2 us
    reduce_scatter x1, waiting for transfers between devices, on_device(): lax.psum_scatter(both, 'tensor', scatter_dimension=0, tiled=True)  44 us
    all_gather x1, waiting for transfers between devices, on_device(): hidden = lax.all_gather(hidden_part, 'tensor', axis=0, tiled=True)  35.5 us
    gather x1, local copies, waits for them, and re-layouts, on_device(): pick = with_zero_row(rows)[unit_list]  33 us
    unnamed x13, local copies, waits for them, and re-layouts  25.7 us
    all_to_all x1, waiting for transfers between devices, on_device(): lax.all_to_all(expert_out, 'dp', split_axis=0, concat_axis=0, tiled=True)  19.6 us
    slice x1, local copies, waits for them, and re-layouts, on_device(): own[:, 2, :]  18.2 us
  transfers between devices with their start and end apart: 6, of which 6 were waited for; matrix products, arithmetic and copies ran while one was open for 9% of the time, Pallas kernels for 0%

profile of v1, /device:TPU:1, one launch (start us, length us, event | category | flops | bytes accessed | tf_op | source)
XLA Modules:
  0.0 451.2 jit_solution(5226104023529939072)
XLA Ops:
  8.6 8.4 %copy.72 = bf16[56,3,8192]{0,1,2:T(4,128)(2,1)} copy(bf16[56,3,8192]{2,0,1:T(8,128)(2,1)S(1)} %pad_maximum_fusion.1) | data formatting | bytes 5505024 | tf_op jit(solution)/shard_map/stack | solution.py:39
  17.0 12.4 %reshape.154 = bf16[8,2,86016]{2,1,0:T(2,128)(2,1)} reshape(bf16[8192,3,56]{2,1,0:T(4,128)(2,1)} %bitcast.87) | data formatting | bytes 5505024
  29.4 9.1 %all-to-all-start.1 = ((bf16[8,2,86016]{2,1,0:T(2,128)(2,1)}), bf16[8,2,86016]{2,1,0:T(2,128)(2,1)S(1)}, u32[]{:S(2)}, u32[]{:S(2)}) async-start(bf16[8,2,86016]{2,1,0:T(2,128)(2,1)} %reshape.154), calls=%async_computation.1 | async-start | bytes 5505024 | tf_op jit(solution)/shard_map/all_to_all | solution.py:40
  40.2 2.9 scatter_custom_fusion.1
  43.1 61.2 %all-to-all-done.1 = bf16[8,2,86016]{2,1,0:T(2,128)(2,1)S(1)} async-done(((bf16[8,2,86016]{2,1,0:T(2,128)(2,1)}), bf16[8,2,86016]{2,1,0:T(2,128)(2,1)S(1)}, u32[]{:S(2)}, u32[]{:S(2)}) %all-to-all-start.1) | async-done | bytes 2752544 | tf_op jit(solution)/shard_map/all_to_all | solution.py:40
  104.3 13.2 %reshape.155 = bf16[8192,3,56]{2,1,0:T(4,128)(2,1)} reshape(bf16[8,2,86016]{2,1,0:T(2,128)(2,1)S(1)} %all-to-all-done.1) | data formatting | bytes 5505024
  117.5 10.6 %copy.79 = bf16[56,3,8,1024]{3,0,2,1:T(8,128)(2,1)S(1)} copy(bf16[56,3,8,1024]{0,1,3,2:T(4,128)(2,1)} %bitcast.88) | data formatting | bytes 5505024 | tf_op jit(solution)/shard_map/all_to_all | solution.py:40
  130.5 3.2 concatenate.7
  133.7 33.0 %gather_fusion.1 = bf16[896,3,1024]{2,1,0:T(4,128)(2,1)} fusion(bf16[449,3,1024]{2,1,0:T(4,128)(2,1)} %concatenate.7, s32[1024]{0:T(1024)S(1)} %pad_clamp_fusion.1), kind=kCustom, calls=%fused_computation.1 | custom fusion | bytes 11013632 | tf_op jit(solution)/shard_map/gather | solution.py:43
  166.7 7.7 %all-to-all-start.2 = ((bf16[896,3,1024]{2,1,0:T(4,128)(2,1)}), bf16[896,3,1024]{2,1,0:T(4,128)(2,1)}, u32[]{:S(2)}, u32[]{:S(2)}) async-start(bf16[896,3,1024]{2,1,0:T(4,128)(2,1)} %gather_fusion.1), calls=%async_computation.2 | async-start | bytes 14680064 | tf_op jit(solution)/shard_map/all_to_all | solution.py:44
  180.3 5.4 %gather_fusion = bf16[1024,1024]{1,0:T(8,128)(2,1)} fusion(bf16[257,1024]{1,0:T(8,128)(2,1)S(1)} %concatenate.6, s32[1024]{0:T(1024)S(1)} %fusion.21), kind=kCustom, calls=%fused_computation | custom fusion | bytes 4198400 | tf_op jit(solution)/shard_map/gather | solution.py:52
  185.7 75.9 %all-to-all-done.2 = bf16[896,3,1024]{2,1,0:T(4,128)(2,1)} async-done(((bf16[896,3,1024]{2,1,0:T(4,128)(2,1)}), bf16[896,3,1024]{2,1,0:T(4,128)(2,1)}, u32[]{:S(2)}, u32[]{:S(2)}) %all-to-all-start.2) | async-done | bytes 5505056 | tf_op jit(solution)/shard_map/all_to_all | solution.py:44
  261.6 8.7 %all-to-all-start = ((bf16[32,32,1024]{2,1,0:T(8,128)(2,1)}), bf16[32,32,1024]{2,1,0:T(8,128)(2,1)S(1)}, u32[]{:S(2)}, u32[]{:S(2)}) async-start(bf16[32,32,1024]{2,1,0:T(8,128)(2,1)} %bitcast.4), calls=%async_computation | async-start | bytes 4194304 | tf_op jit(solution)/shard_map/all_to_all | solution.py:53
  270.3 18.2 %fusion.28 = (bf16[896,1,1024]{2,1,0:T(2,128)(2,1)}, bf16[896,1,1024]{2,1,0:T(2,128)(2,1)}, bf16[896,1,1024]{2,1,0:T(2,128)(2,1)}) fusion(bf16[896,3,1024]{2,1,0:T(4,128)(2,1)} %all-to-all-done.2), kind=kLoop, calls=%fused_computation.70 | loop fusion | bytes 11010048 | tf_op jit(solution)/shard_map/slice | solution.py:61
  288.6 10.0 %all-to-all-done = bf16[32,32,1024]{2,1,0:T(8,128)(2,1)S(1)} async-done(((bf16[32,32,1024]{2,1,0:T(8,128)(2,1)}), bf16[32,32,1024]{2,1,0:T(8,128)(2,1)S(1)}, u32[]{:S(2)}, u32[]{:S(2)}) %all-to-all-start) | async-done | bytes 2097184 | tf_op jit(solution)/shard_map/all_to_all | solution.py:53
  298.6 4.6 %convert_bitcast_fusion.1 = bf16[1024,1,896]{2,0,1:T(8,128)(2,1)S(1)} fusion(bf16[1024,1024]{1,0:T(8,128)(2,1)S(1)} %bitcast.91, bf16[896,1,1024]{2,1,0:T(2,128)(2,1)} %get-tuple-element.9), kind=kOutput, calls=%fused_computation.19 | convolution fusion | flops 1879965696 | bytes 5767168 | tf_op jit(solution)/shard_map/dot_general | solution.py:24
  307.8 44.0 %reduce-scatter.2.cloned.1.call-done = bf16[128,2,896]{2,0,1:T(8,128)(2,1)} async-done(((bf16[1024,2,896]{2,0,1:T(8,128)(2,1)}), bf16[128,2,896]{2,0,1:T(8,128)(2,1)}) %reduce-scatter.2.cloned.1.call-update) | async-done | bytes 458768 | tf_op jit(solution)/shard_map/reduce_scatter | solution.py:58
  353.8 35.5 %all-gather.2.cloned.1.call-done = bf16[1024,896]{1,0:T(8,128)(2,1)} async-done(((bf16[128,896]{1,0:T(8,128)(2,1)}), bf16[1024,896]{1,0:T(8,128)(2,1)}) %all-gather.2.cloned.1.call-update) | async-done | bytes 1835024 | tf_op jit(solution)/shard_map/all_gather | solution.py:60
  389.2 6.3 %convolution_convert_fusion = bf16[1024,1024]{1,0:T(8,128)(2,1)} fusion(bf16[1024,896]{1,0:T(8,128)(2,1)} %all-gather.2.cloned.1.call-done, bf16[896,1,1024]{2,1,0:T(2,128)(2,1)} %get-tuple-element.7), kind=kOutput, calls=%fused_computation.9 | convolution fusion | flops 1880096768 | bytes 5767168 | tf_op jit(solution)/shard_map/dot_general | solution.py:61
  395.6 11.6 %all-to-all-start.3 = ((bf16[32,32,1024]{2,1,0:T(8,128)(2,1)}), bf16[32,32,1024]{2,1,0:T(8,128)(2,1)S(1)}, u32[]{:S(2)}, u32[]{:S(2)}) async-start(bf16[32,32,1024]{2,1,0:T(8,128)(2,1)} %bitcast.90), calls=%async_computation.4 | async-start | bytes 4194304 | tf_op jit(solution)/shard_map/all_to_all | solution.py:62
  407.5 3.5 fusion.29
  411.1 4.5 %gather_fusion.3 = f32[512]{0:T(512)S(1)} fusion(f32[256,32]{0,1:T(8,128)S(1)} %fusion.29, s32[512]{0:T(512)S(1)} %reshape.119), kind=kCustom, calls=%fused_computation.3 | custom fusion | bytes 8192 | tf_op jit(solution)/shard_map/jit(take_along_axis)/gather | solution.py:36
  416.1 19.6 %all-to-all-done.3 = bf16[32,32,1024]{2,1,0:T(8,128)(2,1)S(1)} async-done(((bf16[32,32,1024]{2,1,0:T(8,128)(2,1)}), bf16[32,32,1024]{2,1,0:T(8,128)(2,1)S(1)}, u32[]{:S(2)}, u32[]{:S(2)}) %all-to-all-start.3) | async-done | bytes 2097184 | tf_op jit(solution)/shard_map/all_to_all | solution.py:62
  440.9 3.5 multiply_reduce_fusion
  (61 shorter events, 24.3 us)
Async XLA Ops:
  6.5 401.0 %copy-start = (bf16[8192,32]{0,1:T(8,128)(2,1)S(1)}, bf16[8192,32]{0,1:T(8,128)(2,1)}, u32[]{:S(2)}) copy-start(bf16[8192,32]{0,1:T(8,128)(2,1)} %param.8) | copy-start | bytes 1572868
  29.4 9.1 %copy-start.4 = (s32[448,1]{0,1:T(1,128)S(1)}, s32[448,1]{0,1:T(1,128)}, u32[]{:S(2)}) copy-start(s32[448,1]{0,1:T(1,128)} %param.12) | copy-start | bytes 5380
  29.4 74.9 %all-to-all-start.1 = ((bf16[8,2,86016]{2,1,0:T(2,128)(2,1)}), bf16[8,2,86016]{2,1,0:T(2,128)(2,1)S(1)}, u32[]{:S(2)}, u32[]{:S(2)}) async-start(bf16[8,2,86016]{2,1,0:T(2,128)(2,1)} %reshape.154), calls=%async_computation.1 | async-start | bytes 5505024 | tf_op jit(solution)/shard_map/all_to_all | solution.py:40
  166.7 7.7 %copy-start.3 = (s32[256,2]{0,1:T(2,128)S(1)}, s32[256,2]{0,1:T(2,128)}, u32[]{:S(2)}) copy-start(s32[256,2]{0,1:T(2,128)} %param.13) | copy-start | bytes 6148
  166.7 94.8 %all-to-all-start.2 = ((bf16[896,3,1024]{2,1,0:T(4,128)(2,1)}), bf16[896,3,1024]{2,1,0:T(4,128)(2,1)}, u32[]{:S(2)}, u32[]{:S(2)}) async-start(bf16[896,3,1024]{2,1,0:T(4,128)(2,1)} %gather_fusion.1), calls=%async_computation.2 | async-start | bytes 14680064 | tf_op jit(solution)/shard_map/all_to_all | solution.py:44
  261.6 37.0 %all-to-all-start = ((bf16[32,32,1024]{2,1,0:T(8,128)(2,1)}), bf16[32,32,1024]{2,1,0:T(8,128)(2,1)S(1)}, u32[]{:S(2)}, u32[]{:S(2)}) async-start(bf16[32,32,1024]{2,1,0:T(8,128)(2,1)} %bitcast.4), calls=%async_computation | async-start | bytes 4194304 | tf_op jit(solution)/shard_map/all_to_all | solution.py:53
  270.3 81.6 %reduce-scatter.2.cloned.1.call-start = ((), (), s32[]{:S(2)}) async-start(), calls=%async_computation.5 | async-start | bytes 4128768 | tf_op jit(solution)/shard_map/reduce_scatter | solution.py:58
  298.6 4.6 %copy-start.2 = (bf16[896,1,1024]{2,1,0:T(2,128)(2,1)S(1)}, bf16[896,1,1024]{2,1,0:T(2,128)(2,1)}, u32[]{:S(2)}) copy-start(bf16[896,1,1024]{2,1,0:T(2,128)(2,1)} %get-tuple-element.8) | copy-start | bytes 5505028
  307.8 81.5 %all-gather.2.cloned.1.call-start = ((), (), s32[]{:S(2)}) async-start(), calls=%async_computation.6 | async-start | bytes 2064384 | tf_op jit(solution)/shard_map/all_gather | solution.py:60
  395.6 40.1 %all-to-all-start.3 = ((bf16[32,32,1024]{2,1,0:T(8,128)(2,1)}), bf16[32,32,1024]{2,1,0:T(8,128)(2,1)S(1)}, u32[]{:S(2)}, u32[]{:S(2)}) async-start(bf16[32,32,1024]{2,1,0:T(8,128)(2,1)} %bitcast.90), calls=%async_computation.4 | async-start | bytes 4194304 | tf_op jit(solution)/shard_map/all_to_all | solution.py:62
  435.7 8.6 %copy-start.1 = (bf16[8192,32]{0,1:T(8,128)(2,1)S(1)}, bf16[8192,32]{0,1:T(8,128)(2,1)}, u32[]{:S(2)}) copy-start(bf16[8192,32]{0,1:T(8,128)(2,1)} %param.8) | copy-start | bytes 1572868
Sparse Core Ops, SparseCore 0:
  307.9 43.9 reduce-scatter.1
  353.9 35.2 all-gather.1
